TPU v7x, 256 devices: a whole 4x4x8 slice. The times are simulated.
256 devices in a mesh: depth: 8 (over y_hi, x), shots: 32 (over z, y_lo, core).
Axes of the slice: x: 4, y: 4 (y_hi: 2, y_lo: 2; y = y_hi * 2 + y_lo), z: 8, core: 2. Of those that a mesh axis runs over, the one named last changes fastest.
Arguments:
- adj_now: float32 [32, 128, 128, 128], P('shots', 'depth'), may hold values from -6 to 6
- adj_prev: float32 [32, 128, 128, 128], P('shots', 'depth'), may hold values from -6 to 6
- fwd_snap: bfloat16 [32, 4, 128, 128, 128], P('shots', None, 'depth'), may hold values from -6 to 6
- velocity: float32 [128, 128, 128], P('depth', 'shots'), may hold values from 1 to 2
- density: float32 [128, 128, 128], P('depth', 'shots'), may hold values from 1 to 2
- shot_count: int32 [32], P('shots'), may hold values from 1 to 12, 128 in all
- rec_x: int32 [32, 256], P('shots'), may hold values from 0 to 127
- rec_y: int32 [32, 256], P('shots'), may hold values from 0 to 127
- residual: float32 [32, 4, 256], P('shots'), may hold values from -6 to 6
Outputs:
- out_now: float32 [32, 128, 128, 128], P('shots', 'depth')
- out_prev: float32 [32, 128, 128, 128], P('shots', 'depth')
- grad_vel: float32 [128, 128, 128], P('depth', 'shots')
Inputs may be any that keep to these rules, and one draw needn't show every extreme that they name: `shot_count`: the counts sum to 128; the largest is exactly 12.
All inputs are finite; a program needn't handle non-finite values.
Results may differ from a plain program's by a relative error of at most 0.0003.
Values sent between devices are 32-bit elements; how exact they have to be, the bound alone decides.
No kernel may reach another device: no remote copies, remote signals or barrier semaphores. Data moves between devices by JAX's collectives and lax.ppermute only.
A program may use at most 64 MiB of HBM per device.

v0:
```python
import jax
import jax.numpy as jnp
from jax import lax
from jax.sharding import PartitionSpec as P


def with_halo(shard, sides, width):
    for axis, dim in sides:
        peers, length = (lax.axis_size(axis), shard.shape[dim])
        up = [(i, (i + 1) % peers) for i in range(peers - 1)]
        down = [(j, i) for i, j in up]
        last = lax.slice_in_dim(shard, length - width, length, axis=dim)
        first = lax.slice_in_dim(shard, 0, width, axis=dim)
        before = lax.ppermute(last, axis, up)
        after = lax.ppermute(first, axis, down)
        shard = jnp.concatenate([before, shard, after], axis=dim)
    return shard


def operate(field, buoy):
    padded = jnp.pad(field, 1)
    bpad = jnp.pad(buoy, 1)
    total = jnp.zeros_like(field)
    for axis in range(3):
        center = [slice(1, -1)] * 3
        ahead = list(center)
        behind = list(center)
        ahead[axis] = slice(2, None)
        behind[axis] = slice(0, -2)
        pc, pa, pb = (padded[tuple(center)], padded[tuple(ahead)], padded[tuple(behind)])
        bc, ba, bb = (bpad[tuple(center)], bpad[tuple(ahead)], bpad[tuple(behind)])
        total = total + 0.5 * (bc + ba) * (pa - pc) - 0.5 * (bb + bc) * (pc - pb)
    return total


def source_plane(rows_x, rows_y, amounts, width_x, width_y):
    onehot_x = (rows_x[:, None] == jnp.arange(width_x, dtype=jnp.int32)[None, :]).astype(
        jnp.float32
    )
    onehot_y = (rows_y[:, None] == jnp.arange(width_y, dtype=jnp.int32)[None, :]).astype(
        jnp.float32
    )
    return jnp.dot((onehot_x * amounts[:, None]).T, onehot_y, precision=lax.Precision.HIGHEST)


def body(adj_now, adj_prev, fwd_snap, velocity, density, shot_count, rec_x, rec_y, residual):
    depth_planes = adj_now.shape[1]
    width_x = adj_now.shape[2]
    width_y = adj_now.shape[3]
    steps = fwd_snap.shape[1]
    groups = lax.axis_size("shots")
    width = 1
    vel_all, rho_all = (
        lax.all_gather(velocity, "shots", axis=1, tiled=True),
        lax.all_gather(density, "shots", axis=1, tiled=True),
    )
    packed = jnp.stack([rho_all * vel_all * vel_all, 1.0 / rho_all])
    extended = with_halo(packed, (("depth", 1),), width)
    buoy_ext = extended[1]
    first = lax.axis_index("depth") * depth_planes
    snaps = fwd_snap[0]
    rows_x = rec_x[0]
    rows_y = rec_y[0]
    image = jnp.zeros((depth_planes, width_x, width_y), jnp.float32)
    kappa_ext = extended[0, width : width + depth_planes]
    global_plane = first + jnp.arange(depth_planes, dtype=jnp.int32)
    at_receivers = (global_plane == 2).astype(jnp.float32)[:, None, None]
    current = adj_now[0]
    older = adj_prev[0]
    for step in range(steps):
        moment = steps - 1 - step
        rimmed_field = with_halo(current[None], (("depth", 1),), 1)[0]
        plane = source_plane(rows_x, rows_y, residual[0, moment], width_x, width_y)
        spread = operate(rimmed_field, buoy_ext)[1:-1]
        newer = (
            2.0 * current - older + 0.08 * kappa_ext * spread + 0.08 * at_receivers * plane[None]
        )
        image = image + snaps[moment].astype(jnp.float32) * newer
        older = current
        current = newer
    weighted = shot_count[0].astype(jnp.float32) * image
    summed = lax.psum_scatter(weighted, "shots", scatter_dimension=1, tiled=True)
    grad_vel = 2.0 * density * velocity * summed / (4.0 * groups)
    return (current[None], older[None], grad_vel)


def solution(mesh):
    in_specs = (
        P("shots", "depth", None, None),
        P("shots", "depth", None, None),
        P("shots", None, "depth", None, None),
        P("depth", "shots", None),
        P("depth", "shots", None),
        P("shots"),
        P("shots", None),
        P("shots", None),
        P("shots", None, None),
    )
    out_specs = (
        P("shots", "depth", None, None),
        P("shots", "depth", None, None),
        P("depth", "shots", None),
    )
    return jax.shard_map(body, mesh=mesh, in_specs=in_specs, out_specs=out_specs, check_vma=False)
```

profile of v0, /device:TPU:2, one launch (start us, length us, event | category | flops | bytes accessed | tf_op | source)
XLA Modules:
  0.0 387.4 jit_solution(11470372513918090008)
XLA Ops:
  7.2 1.4 copy.15
  8.7 1.4 copy.14
  11.0 4.2 %collective-permute-start.3 = (f32[1,1,128,128]{3,1,2,0:T(1,128)S(1)}, f32[1,1,128,128]{3,1,2,0:T(1,128)S(1)}, u32[]{:S(2)}, u32[]{:S(2)}) collective-permute-start(f32[1,1,128,128]{3,1,2,0:T(1,128)S(1)} %bitcast.68), channel_id=1, source_target_pairs={{32,0},{64,32},{96,64},{128,96},{160,128},{192,160},{224,192},{33,... | collective-permute-start | bytes 196616 | tf_op jit(solution)/shard_map/ppermute | solution.py:15
  15.2 1.9 collective-permute-start.2
  17.1 1.8 copy.12
  19.4 2.9 fusion.102
  22.6 54.4 %all-gather.5.cloned.1.call-done = f32[16,128,128]{2,0,1:T(8,128)} async-done(((f32[16,4,128]{2,0,1:T(8,128)}), f32[16,128,128]{2,0,1:T(8,128)}) %all-gather.5.cloned.1.call-update) | async-done | bytes 1048592 | tf_op jit(solution)/shard_map/all_gather | solution.py:54
  77.0 65.7 %all-gather.3.cloned.1.call-done = f32[16,128,128]{2,0,1:T(8,128)} async-done(((f32[16,4,128]{2,0,1:T(8,128)}), f32[16,128,128]{2,0,1:T(8,128)}) %all-gather.3.cloned.1.call-update) | async-done | bytes 1048592 | tf_op jit(solution)/shard_map/all_gather | solution.py:55
  142.7 1.7 multiply_multiply_fusion
  144.6 2.5 collective-permute-start.1
  147.1 3.4 collective-permute-start
  150.5 4.5 %fusion.12 = (f32[18,128,128]{2,0,1:T(8,128)}, f32[18,128,128]{2,0,1:T(8,128)}, f32[18,128,128]{2,0,1:T(8,128)}, f32[18,128,128]{2,0,1:T(8,128)}, f32[18,128,128]{2,0,1:T(8,128)}, /*index=5*/f32[18,128,128]{2,0,1:T(8,128)}) fusion(f32[18,128,128]{2,0,1:T(8,128)S(1)} %maximum_bitcast_fusion), kind=kLoop, calls=%fused_computation.42 | loop fusion | flops 589824 | bytes 8257536 | tf_op jit(solution)/shard_map/sub | solution.py:32
  157.6 1.5 copy-done.6
  161.0 4.0 %fusion.61 = f32[16,128,128]{2,0,1:T(8,128)S(1)} fusion(f32[18,128,128]{2,0,1:T(8,128)S(1)} %copy-done.9, f32[18,128,128]{2,0,1:T(8,128)S(1)} %copy-done.8, f32[18,128,128]{2,0,1:T(8,128)S(1)} %copy-done.7, f32[18,128,128]{2,0,1:T(8,128)S(1)} %copy-done.11, f32[18,128,128]{2,0,1:T(8,128)S(1)} %copy-done.4, f32[18,128,128]{2,0,1:T(8,128)S(1)} %copy-done.10, ...), kind=kLoop, calls=%fused_computation.118 | loop fusion | flops 5767168 | bytes 17891392 | tf_op jit(solution)/shard_map/add | solution.py:76
  165.1 2.5 collective-permute-start.5
  167.6 3.4 collective-permute-start.4
  171.4 2.4 collective-permute-done.4
  173.7 1.4 maximum_bitcast_fusion.1
  175.1 10.0 %fusion.14 = (f32[18,128,128]{2,0,1:T(8,128)}, f32[18,128,128]{2,0,1:T(8,128)}, f32[18,128,128]{2,0,1:T(8,128)}, f32[18,128,128]{2,0,1:T(8,128)}, f32[18,128,128]{2,0,1:T(8,128)}, /*index=5*/f32[18,128,128]{2,0,1:T(8,128)}) fusion(f32[18,128,128]{2,0,1:T(8,128)} %maximum_bitcast_fusion.1), kind=kLoop, calls=%fused_computation.44 | loop fusion | flops 589824 | bytes 8257536 | tf_op jit(solution)/shard_map/sub | solution.py:32
  185.1 6.6 %fusion.49 = f32[16,128,128]{2,0,1:T(8,128)S(1)} fusion(f32[18,128,128]{2,0,1:T(8,128)} %get-tuple-element.29, f32[18,128,128]{2,0,1:T(8,128)} %get-tuple-element.28, f32[18,128,128]{2,0,1:T(8,128)} %get-tuple-element.27, f32[18,128,128]{2,0,1:T(8,128)} %get-tuple-element.31, f32[18,128,128]{2,0,1:T(8,128)} %maximum_bitcast_fusion.1, ...), kind=kLoop, calls=%fused_computation.100 | loop fusion | flops 5767168 | bytes 17891392 | tf_op jit(solution)/shard_map/add | solution.py:76
  191.8 1.9 collective-permute-start.7
  193.7 5.4 %collective-permute-start.6 = (f32[1,1,128,128]{3,1,2,0:T(1,128)S(1)}, f32[1,1,128,128]{3,1,2,0:T(1,128)S(1)}, u32[]{:S(2)}, u32[]{:S(2)}) collective-permute-start(f32[1,1,128,128]{3,1,2,0:T(1,128)S(1)} %get-tuple-element.46), channel_id=1, source_target_pairs={{0,32},{32,64},{64,96},{96,128},{128,160},{160,192},{192,224},{1,3... | collective-permute-start | bytes 196616 | tf_op jit(solution)/shard_map/ppermute | solution.py:14
  200.9 1.4 maximum_bitcast_fusion.2
  202.3 10.0 %fusion.16 = (f32[18,128,128]{2,0,1:T(8,128)}, f32[18,128,128]{2,0,1:T(8,128)}, f32[18,128,128]{2,0,1:T(8,128)}, f32[18,128,128]{2,0,1:T(8,128)}, f32[18,128,128]{2,0,1:T(8,128)}, /*index=5*/f32[18,128,128]{2,0,1:T(8,128)}) fusion(f32[18,128,128]{2,0,1:T(8,128)} %maximum_bitcast_fusion.2), kind=kLoop, calls=%fused_computation.46 | loop fusion | flops 589824 | bytes 8257536 | tf_op jit(solution)/shard_map/sub | solution.py:32
  212.3 6.5 %fusion.37 = f32[16,128,128]{2,0,1:T(8,128)S(1)} fusion(f32[18,128,128]{2,0,1:T(8,128)} %get-tuple-element.23, f32[18,128,128]{2,0,1:T(8,128)} %get-tuple-element.22, f32[18,128,128]{2,0,1:T(8,128)} %get-tuple-element.21, f32[18,128,128]{2,0,1:T(8,128)} %get-tuple-element.25, f32[18,128,128]{2,0,1:T(8,128)} %maximum_bitcast_fusion.2, ...), kind=kLoop, calls=%fused_computation.82 | loop fusion | flops 5767168 | bytes 17891392 | tf_op jit(solution)/shard_map/add | solution.py:76
  218.9 1.9 collective-permute-start.9
  220.9 7.5 %collective-permute-start.8 = (f32[1,1,128,128]{3,1,2,0:T(1,128)S(1)}, f32[1,1,128,128]{3,1,2,0:T(1,128)S(1)}, u32[]{:S(2)}, u32[]{:S(2)}) collective-permute-start(f32[1,1,128,128]{3,1,2,0:T(1,128)S(1)} %get-tuple-element.44), channel_id=1, source_target_pairs={{0,32},{32,64},{64,96},{96,128},{128,160},{160,192},{192,224},{1,3... | collective-permute-start | bytes 196616 | tf_op jit(solution)/shard_map/ppermute | solution.py:14
  230.3 1.4 maximum_bitcast_fusion.3
  231.7 10.0 %fusion.18 = (f32[18,128,128]{2,0,1:T(8,128)}, f32[18,128,128]{2,0,1:T(8,128)}, f32[18,128,128]{2,0,1:T(8,128)}, f32[18,128,128]{2,0,1:T(8,128)}, f32[18,128,128]{2,0,1:T(8,128)}, /*index=5*/f32[18,128,128]{2,0,1:T(8,128)}) fusion(f32[18,128,128]{2,0,1:T(8,128)} %maximum_bitcast_fusion.3), kind=kLoop, calls=%fused_computation.48 | loop fusion | flops 589824 | bytes 8257536 | tf_op jit(solution)/shard_map/sub | solution.py:32
  241.7 9.0 %fusion.70 = (f32[16,128,128]{2,0,1:T(8,128)}, f32[16,128,128]{2,0,1:T(8,128)}) fusion(f32[16,128,128]{2,0,1:T(8,128)S(1)} %fusion.37, f32[16,128,128]{2,0,1:T(8,128)} %copy-done.2, f32[16,128,128]{2,0,1:T(8,128)S(1)} %fusion.61, bf16[1,1,16,128,128]{4,3,2,1,0:T(8,128)(2,1)} %get-tuple-element.11, bf16[1,1,16,128,128]{4,3,2,1,0:T(8,128)(2,1)} %get-tuple-element.9, ...), kind=kLoop, calls=%fused_computation.133 | loop fusion | flops 8912896 | bytes 22085700 | tf_op jit(solution)/shard_map/mul | solution.py:81
  250.7 1.3 copy.26
  253.3 126.2 %reduce-scatter.2.cloned.1.call-done = f32[16,4,128]{2,0,1:T(8,128)} async-done(((f32[16,128,128]{2,0,1:T(8,128)}), f32[16,4,128]{2,0,1:T(8,128)}) %reduce-scatter.2.cloned.1.call-update) | async-done | bytes 32784 | tf_op jit(solution)/shard_map/reduce_scatter | solution.py:82
  (69 shorter events, 12.6 us)
Async XLA Ops:
  7.2 11.8 %copy-start.16 = (f32[1,4,256]{2,1,0:T(4,128)S(1)}, f32[1,4,256]{2,1,0:T(4,128)}, u32[]{:S(2)}) copy-start(f32[1,4,256]{2,1,0:T(4,128)} %param.17) | copy-start | bytes 12292
  7.2 11.8 %copy-start.17 = (s32[1,256]{1,0:T(1,128)S(1)}, s32[1,256]{1,0:T(1,128)}, u32[]{:S(2)}) copy-start(s32[1,256]{1,0:T(1,128)} %param.16) | copy-start | bytes 3076
  7.2 11.8 %copy-start.18 = (s32[1,256]{1,0:T(1,128)S(1)}, s32[1,256]{1,0:T(1,128)}, u32[]{:S(2)}) copy-start(s32[1,256]{1,0:T(1,128)} %param.15) | copy-start | bytes 3076
  7.2 69.8 %all-gather.5.cloned.1.call-start = ((), (), s32[]{:S(2)}) async-start(), calls=%async_computation.2 | async-start | bytes 1081344 | tf_op jit(solution)/shard_map/all_gather | solution.py:54
  8.6 134.0 %all-gather.3.cloned.1.call-start = ((), (), s32[]{:S(2)}) async-start(), calls=%async_computation.1 | async-start | bytes 1081344 | tf_op jit(solution)/shard_map/all_gather | solution.py:55
  10.1 369.4 %reduce-scatter.2.cloned.1.call-start = ((), (), s32[]{:S(2)}) async-start(), calls=%async_computation.3 | async-start | bytes 1081344 | tf_op jit(solution)/shard_map/reduce_scatter | solution.py:82
  11.0 11.3 %collective-permute-start.3 = (f32[1,1,128,128]{3,1,2,0:T(1,128)S(1)}, f32[1,1,128,128]{3,1,2,0:T(1,128)S(1)}, u32[]{:S(2)}, u32[]{:S(2)}) collective-permute-start(f32[1,1,128,128]{3,1,2,0:T(1,128)S(1)} %bitcast.68), channel_id=1, source_target_pairs={{32,0},{64,32},{96,64},{128,96},{160,128},{192,160},{224,192},{33,... | collective-permute-start | bytes 196616 | tf_op jit(solution)/shard_map/ppermute | solution.py:15
  15.2 7.1 %collective-permute-start.2 = (f32[1,1,128,128]{3,1,2,0:T(1,128)S(1)}, f32[1,1,128,128]{3,1,2,0:T(1,128)S(1)}, u32[]{:S(2)}, u32[]{:S(2)}) collective-permute-start(f32[1,1,128,128]{3,1,2,0:T(1,128)S(1)} %bitcast.67), channel_id=1, source_target_pairs={{0,32},{32,64},{64,96},{96,128},{128,160},{160,192},{192,224},{1,3... | collective-permute-start | bytes 196616 | tf_op jit(solution)/shard_map/ppermute | solution.py:14
  22.6 127.9 %copy-start.3 = (f32[18,128,128]{2,0,1:T(8,128)}, f32[18,128,128]{2,0,1:T(8,128)S(1)}, u32[]{:S(2)}) copy-start(f32[18,128,128]{2,0,1:T(8,128)S(1)} %maximum_bitcast_fusion) | copy-start | bytes 3538948
  144.6 10.4 %collective-permute-start.1 = (f32[2,1,128,128]{3,1,2,0:T(1,128)S(1)}, f32[2,1,128,128]{3,1,2,0:T(1,128)S(1)}, u32[]{:S(2)}, u32[]{:S(2)}) collective-permute-start(f32[2,1,128,128]{3,1,2,0:T(1,128)S(1)} %get-tuple-element.13), channel_id=1, source_target_pairs={{32,0},{64,32},{96,64},{128,96},{160,128},{192,160},{224,192},{33,... | collective-permute-start | bytes 393224 | tf_op jit(solution)/shard_map/ppermute | solution.py:15
  147.1 7.9 %collective-permute-start = (f32[2,1,128,128]{3,1,2,0:T(1,128)S(1)}, f32[2,1,128,128]{3,1,2,0:T(1,128)S(1)}, u32[]{:S(2)}, u32[]{:S(2)}) collective-permute-start(f32[2,1,128,128]{3,1,2,0:T(1,128)S(1)} %get-tuple-element.12), channel_id=1, source_target_pairs={{0,32},{32,64},{64,96},{96,128},{128,160},{160,192},{192,224},{1,3... | collective-permute-start | bytes 393224 | tf_op jit(solution)/shard_map/ppermute | solution.py:14
  155.0 1.6 copy-start.11
  155.0 1.7 copy-start.13
  155.3 2.0 copy-start.4
  155.3 2.3 copy-start.5
  155.3 3.7 copy-start.6
  155.3 4.3 %copy-start.7 = (f32[18,128,128]{2,0,1:T(8,128)S(1)}, f32[18,128,128]{2,0,1:T(8,128)}, u32[]{:S(2)}) copy-start(f32[18,128,128]{2,0,1:T(8,128)} %get-tuple-element.39) | copy-start | bytes 3538948
  155.3 4.8 %copy-start.8 = (f32[18,128,128]{2,0,1:T(8,128)S(1)}, f32[18,128,128]{2,0,1:T(8,128)}, u32[]{:S(2)}) copy-start(f32[18,128,128]{2,0,1:T(8,128)} %get-tuple-element.40) | copy-start | bytes 3538948
  155.3 5.2 %copy-start.9 = (f32[18,128,128]{2,0,1:T(8,128)S(1)}, f32[18,128,128]{2,0,1:T(8,128)}, u32[]{:S(2)}) copy-start(f32[18,128,128]{2,0,1:T(8,128)} %get-tuple-element.41) | copy-start | bytes 3538948
  155.3 5.7 %copy-start.10 = (f32[18,128,128]{2,0,1:T(8,128)S(1)}, f32[18,128,128]{2,0,1:T(8,128)}, u32[]{:S(2)}) copy-start(f32[18,128,128]{2,0,1:T(8,128)} %get-tuple-element.42) | copy-start | bytes 3538948
  156.6 8.3 %copy-start = (f32[18,128,128]{2,0,1:T(8,128)}, f32[18,128,128]{2,0,1:T(8,128)S(1)}, u32[]{:S(2)}) copy-start(f32[18,128,128]{2,0,1:T(8,128)S(1)} %get-tuple-element.36) | copy-start | bytes 3538948
  156.6 8.3 %copy-start.1 = (f32[18,128,128]{2,0,1:T(8,128)}, f32[18,128,128]{2,0,1:T(8,128)S(1)}, u32[]{:S(2)}) copy-start(f32[18,128,128]{2,0,1:T(8,128)S(1)} %get-tuple-element.37) | copy-start | bytes 3538948
  165.1 6.3 %collective-permute-start.5 = (f32[1,1,128,128]{3,1,2,0:T(1,128)S(1)}, f32[1,1,128,128]{3,1,2,0:T(1,128)S(1)}, u32[]{:S(2)}, u32[]{:S(2)}) collective-permute-start(f32[1,1,128,128]{3,1,2,0:T(1,128)S(1)} %get-tuple-element.49), channel_id=1, source_target_pairs={{32,0},{64,32},{96,64},{128,96},{160,128},{192,160},{224,192},{33,... | collective-permute-start | bytes 196616 | tf_op jit(solution)/shard_map/ppermute | solution.py:15
  167.6 6.2 %collective-permute-start.4 = (f32[1,1,128,128]{3,1,2,0:T(1,128)S(1)}, f32[1,1,128,128]{3,1,2,0:T(1,128)S(1)}, u32[]{:S(2)}, u32[]{:S(2)}) collective-permute-start(f32[1,1,128,128]{3,1,2,0:T(1,128)S(1)} %get-tuple-element.48), channel_id=1, source_target_pairs={{0,32},{32,64},{64,96},{96,128},{128,160},{160,192},{192,224},{1,3... | collective-permute-start | bytes 196616 | tf_op jit(solution)/shard_map/ppermute | solution.py:14
  191.7 9.2 %copy-start.2 = (f32[16,128,128]{2,0,1:T(8,128)}, f32[16,128,128]{2,0,1:T(8,128)S(1)}, u32[]{:S(2)}) copy-start(f32[16,128,128]{2,0,1:T(8,128)S(1)} %fusion.49) | copy-start | bytes 3145732
  191.8 7.8 %collective-permute-start.7 = (f32[1,1,128,128]{3,1,2,0:T(1,128)S(1)}, f32[1,1,128,128]{3,1,2,0:T(1,128)S(1)}, u32[]{:S(2)}, u32[]{:S(2)}) collective-permute-start(f32[1,1,128,128]{3,1,2,0:T(1,128)S(1)} %get-tuple-element.47), channel_id=1, source_target_pairs={{32,0},{64,32},{96,64},{128,96},{160,128},{192,160},{224,192},{33,... | collective-permute-start | bytes 196616 | tf_op jit(solution)/shard_map/ppermute | solution.py:15
  193.7 7.1 %collective-permute-start.6 = (f32[1,1,128,128]{3,1,2,0:T(1,128)S(1)}, f32[1,1,128,128]{3,1,2,0:T(1,128)S(1)}, u32[]{:S(2)}, u32[]{:S(2)}) collective-permute-start(f32[1,1,128,128]{3,1,2,0:T(1,128)S(1)} %get-tuple-element.46), channel_id=1, source_target_pairs={{0,32},{32,64},{64,96},{96,128},{128,160},{160,192},{192,224},{1,3... | collective-permute-start | bytes 196616 | tf_op jit(solution)/shard_map/ppermute | solution.py:14
  218.9 10.5 %collective-permute-start.9 = (f32[1,1,128,128]{3,1,2,0:T(1,128)S(1)}, f32[1,1,128,128]{3,1,2,0:T(1,128)S(1)}, u32[]{:S(2)}, u32[]{:S(2)}) collective-permute-start(f32[1,1,128,128]{3,1,2,0:T(1,128)S(1)} %get-tuple-element.45), channel_id=1, source_target_pairs={{32,0},{64,32},{96,64},{128,96},{160,128},{192,160},{224,192},{33,... | collective-permute-start | bytes 196616 | tf_op jit(solution)/shard_map/ppermute | solution.py:15
  220.9 9.4 %collective-permute-start.8 = (f32[1,1,128,128]{3,1,2,0:T(1,128)S(1)}, f32[1,1,128,128]{3,1,2,0:T(1,128)S(1)}, u32[]{:S(2)}, u32[]{:S(2)}) collective-permute-start(f32[1,1,128,128]{3,1,2,0:T(1,128)S(1)} %get-tuple-element.44), channel_id=1, source_target_pairs={{0,32},{32,64},{64,96},{96,128},{128,160},{160,192},{192,224},{1,3... | collective-permute-start | bytes 196616 | tf_op jit(solution)/shard_map/ppermute | solution.py:14
  250.6 1.3 copy-start.12
  252.0 127.5 %copy-start.14 = (f32[16,4,128]{2,1,0:T(4,128)S(1)}, f32[16,4,128]{2,1,0:T(4,128)}, u32[]{:S(2)}) copy-start(f32[16,4,128]{2,1,0:T(4,128)} %param.12) | copy-start | bytes 98308
  252.0 127.5 %copy-start.15 = (f32[16,4,128]{2,1,0:T(4,128)S(1)}, f32[16,4,128]{2,1,0:T(4,128)}, u32[]{:S(2)}) copy-start(f32[16,4,128]{2,1,0:T(4,128)} %param.13) | copy-start | bytes 98308
Sparse Core Ops, SparseCore 0:
  10.4 66.4 all-gather.4
  79.4 63.2 all-gather.2
  250.8 128.6 reduce-scatter.1
where the time goes:
time: 388 us; the launch traced here: 387 us
  waiting for transfers between devices  251 us (65%)
  other arithmetic  69.2 us (18%)
  starting transfers between devices  34.7 us (9%)
  local copies, waits for them, and re-layouts  16.3 us (4%)
  between operations  14.9 us (4%)
    reduce_scatter x1, waiting for transfers between devices, body(): lax.psum_scatter(weighted, 'shots', scatter_dimension=1, tiled=True)  126 us
    all_gather x1, waiting for transfers between devices, body(): lax.all_gather(density, 'shots', axis=1, tiled=True)  65.7 us
    all_gather x1, waiting for transfers between devices, body(): lax.all_gather(velocity, 'shots', axis=1, tiled=True)  54.4 us
    sub x4, other arithmetic, operate(): total = total + 0.5 * (bc + ba) * (pa - pc) - 0.5 * (bb + bc) * (pc - pb)  34.5 us
    ppermute x5, starting transfers between devices, with_halo(): before = lax.ppermute(last, axis, up)  21.6 us
    add x3, other arithmetic, body(): 2.0 * current - older + 0.08 * kappa_ext * spread  17.1 us
    ppermute x5, starting transfers between devices, with_halo(): after = lax.ppermute(first, axis, down)  12.9 us
    unnamed x44, local copies, waits for them, and re-layouts  12.2 us
  transfers between devices with their start and end apart: 13, of which 6 were waited for; matrix products, arithmetic and copies ran while one was open for 4% of the time, Pallas kernels for 0%

commit v1 on v0

--- a/solution.py
+++ b/solution.py
@@ -51,7 +51,9 @@
     groups = lax.axis_size("shots")
     width = 1
     vel_all, rho_all = (
-        lax.all_gather(velocity, "shots", axis=1, tiled=True),
+        jnp.concatenate(
+            lax.all_to_all(jnp.stack([velocity] * lax.axis_size("shots")), "shots", 0, 0), axis=1
+        ),
         lax.all_gather(density, "shots", axis=1, tiled=True),
     )
     packed = jnp.stack([rho_all * vel_all * vel_all, 1.0 / rho_all])

time: 388 us -> 333 us (0.86)
  waiting for transfers between devices: 251 us -> 186 us
  starting transfers between devices: 34.7 us -> 44.5 us
    all_gather x1 -> x0, waiting for transfers between devices: 54.4 us -> none  [body(): lax.all_gather(velocity, 'shots', axis=1, tiled=True)]
    all_gather x1, waiting for transfers between devices: 65.7 us -> 37 us  [body(): lax.all_gather(density, 'shots', axis=1, tiled=True)]
    all_to_all x0 -> x1, waiting for transfers between devices: none -> 18.5 us  [body(): lax.all_to_all(jnp.stack([velocity] * lax.axis_size('shots')), 'shots', 0...]
    all_to_all x0 -> x1, starting transfers between devices: none -> 10 us  [body(): lax.all_to_all(jnp.stack([velocity] * lax.axis_size('shots')), 'shots', 0...]
    unnamed x44 -> x49, local copies, waits for them, and re-layouts: 12.2 us -> 10.3 us
where the time goes in v1:
time: 333 us
  waiting for transfers between devices  186 us (56%)
  other arithmetic  69.3 us (21%)
  starting transfers between devices  44.5 us (13%)
  local copies, waits for them, and re-layouts  16.3 us (5%)
  between operations  15.2 us (5%)
    reduce_scatter x1, waiting for transfers between devices, body(): lax.psum_scatter(weighted, 'shots', scatter_dimension=1, tiled=True)  126 us
    all_gather x1, waiting for transfers between devices, body(): lax.all_gather(density, 'shots', axis=1, tiled=True)  37 us
    sub x4, other arithmetic, operate(): total = total + 0.5 * (bc + ba) * (pa - pc) - 0.5 * (bb + bc) * (pc - pb)  34.7 us
    ppermute x5, starting transfers between devices, with_halo(): before = lax.ppermute(last, axis, up)  23.3 us
    all_to_all x1, waiting for transfers between devices, body(): lax.all_to_all(jnp.stack([velocity] * lax.axis_size('shots')), 'shots', 0...  18.5 us
    add x3, other arithmetic, body(): 2.0 * current - older + 0.08 * kappa_ext * spread  17 us
    ppermute x5, starting transfers between devices, with_halo(): after = lax.ppermute(first, axis, down)  11.1 us
    unnamed x49, local copies, waits for them, and re-layouts  10.3 us
  transfers between devices with their start and end apart: 13, of which 6 were waited for; matrix products, arithmetic and copies ran while one was open for 4% of the time, Pallas kernels for 0%

profile of v1, /device:TPU:2, one launch (start us, length us, event | category | flops | bytes accessed | tf_op | source)
XLA Modules:
  0.0 332.6 jit_solution(8144369450489569510)
XLA Ops:
  7.2 2.1 stack.8
  9.2 10.0 %all-to-all-start = ((f32[32,16,4,128]{3,2,1,0:T(4,128)}), f32[32,16,4,128]{3,2,1,0:T(4,128)}, u32[]{:S(2)}, u32[]{:S(2)}) async-start(f32[32,16,4,128]{3,2,1,0:T(4,128)} %stack.8), calls=%async_computation | async-start | bytes 2097152 | tf_op jit(solution)/shard_map/all_to_all | solution.py:55
  20.1 2.4 collective-permute-start.3
  22.6 3.4 %collective-permute-start.2 = (f32[1,1,128,128]{3,1,2,0:T(1,128)S(1)}, f32[1,1,128,128]{3,1,2,0:T(1,128)S(1)}, u32[]{:S(2)}, u32[]{:S(2)}) collective-permute-start(f32[1,1,128,128]{3,1,2,0:T(1,128)S(1)} %bitcast.70), channel_id=1, source_target_pairs={{0,32},{32,64},{64,96},{96,128},{128,160},{160,192},{192,224},{1,3... | collective-permute-start | bytes 196616 | tf_op jit(solution)/shard_map/ppermute | solution.py:14
  26.0 1.6 copy.12
  28.0 1.3 fusion.104
  30.1 18.5 %all-to-all-done = f32[32,16,4,128]{3,2,1,0:T(4,128)} async-done(((f32[32,16,4,128]{3,2,1,0:T(4,128)}), f32[32,16,4,128]{3,2,1,0:T(4,128)}, u32[]{:S(2)}, u32[]{:S(2)}) %all-to-all-start) | async-done | bytes 1048608 | tf_op jit(solution)/shard_map/all_to_all | solution.py:55
  48.5 2.3 copy.15
  50.8 37.0 %all-gather.2.cloned.1.call-done = f32[16,128,128]{2,0,1:T(8,128)} async-done(((f32[16,4,128]{2,0,1:T(8,128)}), f32[16,128,128]{2,0,1:T(8,128)}) %all-gather.2.cloned.1.call-update) | async-done | bytes 1048592 | tf_op jit(solution)/shard_map/all_gather | solution.py:57
  87.9 1.7 multiply_multiply_fusion
  89.8 2.4 collective-permute-start.1
  92.2 3.4 %collective-permute-start = (f32[2,1,128,128]{3,1,2,0:T(1,128)S(1)}, f32[2,1,128,128]{3,1,2,0:T(1,128)S(1)}, u32[]{:S(2)}, u32[]{:S(2)}) collective-permute-start(f32[2,1,128,128]{3,1,2,0:T(1,128)S(1)} %get-tuple-element.12), channel_id=1, source_target_pairs={{0,32},{32,64},{64,96},{96,128},{128,160},{160,192},{192,224},{1,3... | collective-permute-start | bytes 393224 | tf_op jit(solution)/shard_map/ppermute | solution.py:14
  95.7 4.5 %fusion.12 = (f32[18,128,128]{2,0,1:T(8,128)}, f32[18,128,128]{2,0,1:T(8,128)}, f32[18,128,128]{2,0,1:T(8,128)}, f32[18,128,128]{2,0,1:T(8,128)}, f32[18,128,128]{2,0,1:T(8,128)}, /*index=5*/f32[18,128,128]{2,0,1:T(8,128)}) fusion(f32[18,128,128]{2,0,1:T(8,128)S(1)} %maximum_bitcast_fusion), kind=kLoop, calls=%fused_computation.42 | loop fusion | flops 589824 | bytes 8257536 | tf_op jit(solution)/shard_map/sub | solution.py:32
  102.8 1.5 copy-done.7
  106.2 3.9 %fusion.61 = f32[16,128,128]{2,0,1:T(8,128)S(1)} fusion(f32[18,128,128]{2,0,1:T(8,128)S(1)} %copy-done.10, f32[18,128,128]{2,0,1:T(8,128)S(1)} %copy-done.9, f32[18,128,128]{2,0,1:T(8,128)S(1)} %copy-done.8, f32[18,128,128]{2,0,1:T(8,128)S(1)} %copy-done.12, f32[18,128,128]{2,0,1:T(8,128)S(1)} %copy-done.4, f32[18,128,128]{2,0,1:T(8,128)S(1)} %copy-done.11, ...), kind=kLoop, calls=%fused_computation.118 | loop fusion | flops 5767168 | bytes 17891392 | tf_op jit(solution)/shard_map/add | solution.py:78
  110.3 2.4 collective-permute-start.5
  112.7 3.4 %collective-permute-start.4 = (f32[1,1,128,128]{3,1,2,0:T(1,128)S(1)}, f32[1,1,128,128]{3,1,2,0:T(1,128)S(1)}, u32[]{:S(2)}, u32[]{:S(2)}) collective-permute-start(f32[1,1,128,128]{3,1,2,0:T(1,128)S(1)} %get-tuple-element.48), channel_id=1, source_target_pairs={{0,32},{32,64},{64,96},{96,128},{128,160},{160,192},{192,224},{1,3... | collective-permute-start | bytes 196616 | tf_op jit(solution)/shard_map/ppermute | solution.py:14
  116.6 2.3 collective-permute-done.4
  118.9 1.4 maximum_bitcast_fusion.1
  120.3 10.1 %fusion.14 = (f32[18,128,128]{2,0,1:T(8,128)}, f32[18,128,128]{2,0,1:T(8,128)}, f32[18,128,128]{2,0,1:T(8,128)}, f32[18,128,128]{2,0,1:T(8,128)}, f32[18,128,128]{2,0,1:T(8,128)}, /*index=5*/f32[18,128,128]{2,0,1:T(8,128)}) fusion(f32[18,128,128]{2,0,1:T(8,128)} %maximum_bitcast_fusion.1), kind=kLoop, calls=%fused_computation.44 | loop fusion | flops 589824 | bytes 8257536 | tf_op jit(solution)/shard_map/sub | solution.py:32
  130.3 6.5 %fusion.49 = f32[16,128,128]{2,0,1:T(8,128)S(1)} fusion(f32[18,128,128]{2,0,1:T(8,128)} %get-tuple-element.29, f32[18,128,128]{2,0,1:T(8,128)} %get-tuple-element.28, f32[18,128,128]{2,0,1:T(8,128)} %get-tuple-element.27, f32[18,128,128]{2,0,1:T(8,128)} %get-tuple-element.31, f32[18,128,128]{2,0,1:T(8,128)} %maximum_bitcast_fusion.1, ...), kind=kLoop, calls=%fused_computation.100 | loop fusion | flops 5767168 | bytes 17891392 | tf_op jit(solution)/shard_map/add | solution.py:78
  137.0 1.9 collective-permute-start.7
  138.9 5.5 %collective-permute-start.6 = (f32[1,1,128,128]{3,1,2,0:T(1,128)S(1)}, f32[1,1,128,128]{3,1,2,0:T(1,128)S(1)}, u32[]{:S(2)}, u32[]{:S(2)}) collective-permute-start(f32[1,1,128,128]{3,1,2,0:T(1,128)S(1)} %get-tuple-element.46), channel_id=1, source_target_pairs={{0,32},{32,64},{64,96},{96,128},{128,160},{160,192},{192,224},{1,3... | collective-permute-start | bytes 196616 | tf_op jit(solution)/shard_map/ppermute | solution.py:14
  146.2 1.4 maximum_bitcast_fusion.2
  147.6 10.1 %fusion.16 = (f32[18,128,128]{2,0,1:T(8,128)}, f32[18,128,128]{2,0,1:T(8,128)}, f32[18,128,128]{2,0,1:T(8,128)}, f32[18,128,128]{2,0,1:T(8,128)}, f32[18,128,128]{2,0,1:T(8,128)}, /*index=5*/f32[18,128,128]{2,0,1:T(8,128)}) fusion(f32[18,128,128]{2,0,1:T(8,128)} %maximum_bitcast_fusion.2), kind=kLoop, calls=%fused_computation.46 | loop fusion | flops 589824 | bytes 8257536 | tf_op jit(solution)/shard_map/sub | solution.py:32
  157.6 6.5 %fusion.37 = f32[16,128,128]{2,0,1:T(8,128)S(1)} fusion(f32[18,128,128]{2,0,1:T(8,128)} %get-tuple-element.23, f32[18,128,128]{2,0,1:T(8,128)} %get-tuple-element.22, f32[18,128,128]{2,0,1:T(8,128)} %get-tuple-element.21, f32[18,128,128]{2,0,1:T(8,128)} %get-tuple-element.25, f32[18,128,128]{2,0,1:T(8,128)} %maximum_bitcast_fusion.2, ...), kind=kLoop, calls=%fused_computation.82 | loop fusion | flops 5767168 | bytes 17891392 | tf_op jit(solution)/shard_map/add | solution.py:78
  164.2 1.9 collective-permute-start.9
  166.2 7.5 %collective-permute-start.8 = (f32[1,1,128,128]{3,1,2,0:T(1,128)S(1)}, f32[1,1,128,128]{3,1,2,0:T(1,128)S(1)}, u32[]{:S(2)}, u32[]{:S(2)}) collective-permute-start(f32[1,1,128,128]{3,1,2,0:T(1,128)S(1)} %get-tuple-element.44), channel_id=1, source_target_pairs={{0,32},{32,64},{64,96},{96,128},{128,160},{160,192},{192,224},{1,3... | collective-permute-start | bytes 196616 | tf_op jit(solution)/shard_map/ppermute | solution.py:14
  175.6 1.4 maximum_bitcast_fusion.3
  177.0 10.1 %fusion.18 = (f32[18,128,128]{2,0,1:T(8,128)}, f32[18,128,128]{2,0,1:T(8,128)}, f32[18,128,128]{2,0,1:T(8,128)}, f32[18,128,128]{2,0,1:T(8,128)}, f32[18,128,128]{2,0,1:T(8,128)}, /*index=5*/f32[18,128,128]{2,0,1:T(8,128)}) fusion(f32[18,128,128]{2,0,1:T(8,128)} %maximum_bitcast_fusion.3), kind=kLoop, calls=%fused_computation.48 | loop fusion | flops 589824 | bytes 8257536 | tf_op jit(solution)/shard_map/sub | solution.py:32
  187.0 8.9 %fusion.70 = (f32[16,128,128]{2,0,1:T(8,128)}, f32[16,128,128]{2,0,1:T(8,128)}) fusion(f32[16,128,128]{2,0,1:T(8,128)S(1)} %fusion.37, f32[16,128,128]{2,0,1:T(8,128)} %copy-done.2, f32[16,128,128]{2,0,1:T(8,128)S(1)} %fusion.61, bf16[1,1,16,128,128]{4,3,2,1,0:T(8,128)(2,1)} %get-tuple-element.11, bf16[1,1,16,128,128]{4,3,2,1,0:T(8,128)(2,1)} %get-tuple-element.9, ...), kind=kLoop, calls=%fused_computation.133 | loop fusion | flops 8912896 | bytes 22085700 | tf_op jit(solution)/shard_map/mul | solution.py:83
  198.6 125.7 %reduce-scatter.2.cloned.1.call-done = f32[16,4,128]{2,0,1:T(8,128)} async-done(((f32[16,128,128]{2,0,1:T(8,128)}), f32[16,4,128]{2,0,1:T(8,128)}) %reduce-scatter.2.cloned.1.call-update) | async-done | bytes 32784 | tf_op jit(solution)/shard_map/reduce_scatter | solution.py:84
  (75 shorter events, 14.2 us)
Async XLA Ops:
  7.2 12.2 %copy-start.18 = (f32[16,4,128]{2,1,0:T(4,128)S(1)}, f32[16,4,128]{2,1,0:T(4,128)}, u32[]{:S(2)}) copy-start(f32[16,4,128]{2,1,0:T(4,128)} %param.13) | copy-start | bytes 98308
  7.2 12.9 %copy-start.5 = (f32[1,16,128,128]{3,2,1,0:T(8,128)S(1)}, f32[1,16,128,128]{3,2,1,0:T(8,128)}, u32[]{:S(2)}) copy-start(f32[1,16,128,128]{3,2,1,0:T(8,128)} %param.9) | copy-start | bytes 3145732
  9.2 39.3 %all-to-all-start = ((f32[32,16,4,128]{3,2,1,0:T(4,128)}), f32[32,16,4,128]{3,2,1,0:T(4,128)}, u32[]{:S(2)}, u32[]{:S(2)}) async-start(f32[32,16,4,128]{3,2,1,0:T(4,128)} %stack.8), calls=%async_computation | async-start | bytes 2097152 | tf_op jit(solution)/shard_map/all_to_all | solution.py:55
  19.2 8.3 %copy-start.19 = (f32[1,4,256]{2,1,0:T(4,128)S(1)}, f32[1,4,256]{2,1,0:T(4,128)}, u32[]{:S(2)}) copy-start(f32[1,4,256]{2,1,0:T(4,128)} %param.17) | copy-start | bytes 12292
  19.3 8.3 %copy-start.20 = (s32[1,256]{1,0:T(1,128)S(1)}, s32[1,256]{1,0:T(1,128)}, u32[]{:S(2)}) copy-start(s32[1,256]{1,0:T(1,128)} %param.16) | copy-start | bytes 3076
  19.3 8.3 %copy-start.21 = (s32[1,256]{1,0:T(1,128)S(1)}, s32[1,256]{1,0:T(1,128)}, u32[]{:S(2)}) copy-start(s32[1,256]{1,0:T(1,128)} %param.15) | copy-start | bytes 3076
  19.3 8.7 %copy-start.15 = (bf16[1,4,16,128,128]{4,3,2,1,0:T(8,128)(2,1)S(1)}, bf16[1,4,16,128,128]{4,3,2,1,0:T(8,128)(2,1)}, u32[]{:S(2)}) copy-start(bf16[1,4,16,128,128]{4,3,2,1,0:T(8,128)(2,1)} %param.11) | copy-start | bytes 6291460
  19.3 68.6 %all-gather.2.cloned.1.call-start = ((), (), s32[]{:S(2)}) async-start(), calls=%async_computation.2 | async-start | bytes 1081344 | tf_op jit(solution)/shard_map/all_gather | solution.py:57
  20.0 304.3 %reduce-scatter.2.cloned.1.call-start = ((), (), s32[]{:S(2)}) async-start(), calls=%async_computation.3 | async-start | bytes 1081344 | tf_op jit(solution)/shard_map/reduce_scatter | solution.py:84
  20.1 9.2 %collective-permute-start.3 = (f32[1,1,128,128]{3,1,2,0:T(1,128)S(1)}, f32[1,1,128,128]{3,1,2,0:T(1,128)S(1)}, u32[]{:S(2)}, u32[]{:S(2)}) collective-permute-start(f32[1,1,128,128]{3,1,2,0:T(1,128)S(1)} %bitcast.71), channel_id=1, source_target_pairs={{32,0},{64,32},{96,64},{128,96},{160,128},{192,160},{224,192},{33,... | collective-permute-start | bytes 196616 | tf_op jit(solution)/shard_map/ppermute | solution.py:15
  22.6 6.8 %collective-permute-start.2 = (f32[1,1,128,128]{3,1,2,0:T(1,128)S(1)}, f32[1,1,128,128]{3,1,2,0:T(1,128)S(1)}, u32[]{:S(2)}, u32[]{:S(2)}) collective-permute-start(f32[1,1,128,128]{3,1,2,0:T(1,128)S(1)} %bitcast.70), channel_id=1, source_target_pairs={{0,32},{32,64},{64,96},{96,128},{128,160},{160,192},{192,224},{1,3... | collective-permute-start | bytes 196616 | tf_op jit(solution)/shard_map/ppermute | solution.py:14
  28.0 1.8 copy-start.14
  30.1 65.6 %copy-start.3 = (f32[18,128,128]{2,0,1:T(8,128)}, f32[18,128,128]{2,0,1:T(8,128)S(1)}, u32[]{:S(2)}) copy-start(f32[18,128,128]{2,0,1:T(8,128)S(1)} %maximum_bitcast_fusion) | copy-start | bytes 3538948
  89.8 10.4 %collective-permute-start.1 = (f32[2,1,128,128]{3,1,2,0:T(1,128)S(1)}, f32[2,1,128,128]{3,1,2,0:T(1,128)S(1)}, u32[]{:S(2)}, u32[]{:S(2)}) collective-permute-start(f32[2,1,128,128]{3,1,2,0:T(1,128)S(1)} %get-tuple-element.13), channel_id=1, source_target_pairs={{32,0},{64,32},{96,64},{128,96},{160,128},{192,160},{224,192},{33,... | collective-permute-start | bytes 393224 | tf_op jit(solution)/shard_map/ppermute | solution.py:15
  92.2 8.0 %collective-permute-start = (f32[2,1,128,128]{3,1,2,0:T(1,128)S(1)}, f32[2,1,128,128]{3,1,2,0:T(1,128)S(1)}, u32[]{:S(2)}, u32[]{:S(2)}) collective-permute-start(f32[2,1,128,128]{3,1,2,0:T(1,128)S(1)} %get-tuple-element.12), channel_id=1, source_target_pairs={{0,32},{32,64},{64,96},{96,128},{128,160},{160,192},{192,224},{1,3... | collective-permute-start | bytes 393224 | tf_op jit(solution)/shard_map/ppermute | solution.py:14
  100.5 2.0 copy-start.4
  100.5 2.3 copy-start.6
  100.5 3.7 %copy-start.7 = (f32[18,128,128]{2,0,1:T(8,128)S(1)}, f32[18,128,128]{2,0,1:T(8,128)}, u32[]{:S(2)}) copy-start(f32[18,128,128]{2,0,1:T(8,128)} %get-tuple-element.38) | copy-start | bytes 3538948
  100.5 4.3 %copy-start.8 = (f32[18,128,128]{2,0,1:T(8,128)S(1)}, f32[18,128,128]{2,0,1:T(8,128)}, u32[]{:S(2)}) copy-start(f32[18,128,128]{2,0,1:T(8,128)} %get-tuple-element.39) | copy-start | bytes 3538948
  100.5 4.8 %copy-start.9 = (f32[18,128,128]{2,0,1:T(8,128)S(1)}, f32[18,128,128]{2,0,1:T(8,128)}, u32[]{:S(2)}) copy-start(f32[18,128,128]{2,0,1:T(8,128)} %get-tuple-element.40) | copy-start | bytes 3538948
  100.5 5.2 %copy-start.10 = (f32[18,128,128]{2,0,1:T(8,128)S(1)}, f32[18,128,128]{2,0,1:T(8,128)}, u32[]{:S(2)}) copy-start(f32[18,128,128]{2,0,1:T(8,128)} %get-tuple-element.41) | copy-start | bytes 3538948
  100.6 5.7 %copy-start.11 = (f32[18,128,128]{2,0,1:T(8,128)S(1)}, f32[18,128,128]{2,0,1:T(8,128)}, u32[]{:S(2)}) copy-start(f32[18,128,128]{2,0,1:T(8,128)} %get-tuple-element.42) | copy-start | bytes 3538948
  101.8 8.3 %copy-start = (f32[18,128,128]{2,0,1:T(8,128)}, f32[18,128,128]{2,0,1:T(8,128)S(1)}, u32[]{:S(2)}) copy-start(f32[18,128,128]{2,0,1:T(8,128)S(1)} %get-tuple-element.36) | copy-start | bytes 3538948
  101.9 8.3 %copy-start.1 = (f32[18,128,128]{2,0,1:T(8,128)}, f32[18,128,128]{2,0,1:T(8,128)S(1)}, u32[]{:S(2)}) copy-start(f32[18,128,128]{2,0,1:T(8,128)S(1)} %get-tuple-element.37) | copy-start | bytes 3538948
  110.3 6.3 %collective-permute-start.5 = (f32[1,1,128,128]{3,1,2,0:T(1,128)S(1)}, f32[1,1,128,128]{3,1,2,0:T(1,128)S(1)}, u32[]{:S(2)}, u32[]{:S(2)}) collective-permute-start(f32[1,1,128,128]{3,1,2,0:T(1,128)S(1)} %get-tuple-element.49), channel_id=1, source_target_pairs={{32,0},{64,32},{96,64},{128,96},{160,128},{192,160},{224,192},{33,... | collective-permute-start | bytes 196616 | tf_op jit(solution)/shard_map/ppermute | solution.py:15
  112.7 6.2 %collective-permute-start.4 = (f32[1,1,128,128]{3,1,2,0:T(1,128)S(1)}, f32[1,1,128,128]{3,1,2,0:T(1,128)S(1)}, u32[]{:S(2)}, u32[]{:S(2)}) collective-permute-start(f32[1,1,128,128]{3,1,2,0:T(1,128)S(1)} %get-tuple-element.48), channel_id=1, source_target_pairs={{0,32},{32,64},{64,96},{96,128},{128,160},{160,192},{192,224},{1,3... | collective-permute-start | bytes 196616 | tf_op jit(solution)/shard_map/ppermute | solution.py:14
  136.9 9.3 %copy-start.2 = (f32[16,128,128]{2,0,1:T(8,128)}, f32[16,128,128]{2,0,1:T(8,128)S(1)}, u32[]{:S(2)}) copy-start(f32[16,128,128]{2,0,1:T(8,128)S(1)} %fusion.49) | copy-start | bytes 3145732
  137.0 7.9 %collective-permute-start.7 = (f32[1,1,128,128]{3,1,2,0:T(1,128)S(1)}, f32[1,1,128,128]{3,1,2,0:T(1,128)S(1)}, u32[]{:S(2)}, u32[]{:S(2)}) collective-permute-start(f32[1,1,128,128]{3,1,2,0:T(1,128)S(1)} %get-tuple-element.47), channel_id=1, source_target_pairs={{32,0},{64,32},{96,64},{128,96},{160,128},{192,160},{224,192},{33,... | collective-permute-start | bytes 196616 | tf_op jit(solution)/shard_map/ppermute | solution.py:15
  138.9 7.2 %collective-permute-start.6 = (f32[1,1,128,128]{3,1,2,0:T(1,128)S(1)}, f32[1,1,128,128]{3,1,2,0:T(1,128)S(1)}, u32[]{:S(2)}, u32[]{:S(2)}) collective-permute-start(f32[1,1,128,128]{3,1,2,0:T(1,128)S(1)} %get-tuple-element.46), channel_id=1, source_target_pairs={{0,32},{32,64},{64,96},{96,128},{128,160},{160,192},{192,224},{1,3... | collective-permute-start | bytes 196616 | tf_op jit(solution)/shard_map/ppermute | solution.py:14
  164.2 10.5 %collective-permute-start.9 = (f32[1,1,128,128]{3,1,2,0:T(1,128)S(1)}, f32[1,1,128,128]{3,1,2,0:T(1,128)S(1)}, u32[]{:S(2)}, u32[]{:S(2)}) collective-permute-start(f32[1,1,128,128]{3,1,2,0:T(1,128)S(1)} %get-tuple-element.45), channel_id=1, source_target_pairs={{32,0},{64,32},{96,64},{128,96},{160,128},{192,160},{224,192},{33,... | collective-permute-start | bytes 196616 | tf_op jit(solution)/shard_map/ppermute | solution.py:15
  166.2 9.4 %collective-permute-start.8 = (f32[1,1,128,128]{3,1,2,0:T(1,128)S(1)}, f32[1,1,128,128]{3,1,2,0:T(1,128)S(1)}, u32[]{:S(2)}, u32[]{:S(2)}) collective-permute-start(f32[1,1,128,128]{3,1,2,0:T(1,128)S(1)} %get-tuple-element.44), channel_id=1, source_target_pairs={{0,32},{32,64},{64,96},{96,128},{128,160},{160,192},{192,224},{1,3... | collective-permute-start | bytes 196616 | tf_op jit(solution)/shard_map/ppermute | solution.py:14
  197.3 127.0 %copy-start.17 = (f32[16,4,128]{2,1,0:T(4,128)S(1)}, f32[16,4,128]{2,1,0:T(4,128)}, u32[]{:S(2)}) copy-start(f32[16,4,128]{2,1,0:T(4,128)} %param.12) | copy-start | bytes 98308
  (3 other events, 4.7 us)
Sparse Core Ops, SparseCore 0:
  22.5 65.2 all-gather.1
  196.1 128.1 reduce-scatter.1
